TPU v7x, 256 devices: a whole 4x4x8 slice. The times are simulated.
256 devices in a mesh: hst: 64 (over x, y, z_lo), chip: 4 (over z_hi, core).
Axes of the slice: x: 4, y: 4, z: 8 (z_hi: 2, z_lo: 4; z = z_hi * 4 + z_lo), core: 2. Of those that a mesh axis runs over, the one named last changes fastest.
Arguments:
- points: bfloat16 [131072, 1024], P(('hst', 'chip')), may hold values from -640 to 640
- assign: int32 [131072], P(('hst', 'chip')), may hold values from 0 to 8191, as said below
Outputs:
- centroids: bfloat16 [8192, 1024], P('hst', 'chip')
- nearest: float32 [131072], P(('hst', 'chip'))
Inputs may be any that keep to these rules, and one draw needn't show every extreme that they name: `assign`: cluster o * 128 + j lies in owner block o. Among the 512 points of one device at most 16 name clusters of any one owner block; in every draw one owner block gets exactly 16 points from every device.
All inputs are finite; a program needn't handle non-finite values.
Results may differ from a plain program's by a relative error of at most 0.0095.
Values may be sent and summed in bfloat16 or wider, within the bound.
No kernel may reach another device: no remote copies, remote signals or barrier semaphores. Data moves between devices by JAX's collectives and lax.ppermute only.
A program may use at most 64 MiB of HBM per device.

v0:
```python
import jax
import jax.numpy as jnp
from jax import lax
from jax.sharding import PartitionSpec as P

K_HOST = 128
CYCLE = 8
EPSILON = 1e-06


def shifted(block, axis, distance):
    devices = range(lax.axis_size(axis))
    route = [((i - distance) % len(devices), i) for i in devices]
    return lax.ppermute(block, axis, route)


def cluster_sums(values, labels, row_count):
    stride = min(row_count, 1024)

    def one_block(offset):
        wanted = offset + jnp.arange(stride, dtype=jnp.int32)
        member = (wanted[:, None] == labels[None, :]).astype(jnp.bfloat16)
        return jnp.dot(member, values, preferred_element_type=jnp.float32)

    offsets = jnp.arange(row_count // stride, dtype=jnp.int32) * stride
    return lax.map(one_block, offsets).reshape(row_count, values.shape[1])


def body(points, assign):
    feature_count = points.shape[1]
    chip_count = lax.axis_size("chip")
    chip_index = lax.axis_index("chip")
    quarter = feature_count // chip_count
    host_points, host_labels = (
        lax.all_gather(points, "chip", axis=0, tiled=True),
        lax.all_gather(assign, "chip", axis=0, tiled=True),
    )
    columns = lax.dynamic_slice_in_dim(host_points, chip_index * quarter, quarter, 1)
    shares = lax.psum_scatter(
        cluster_sums(columns, host_labels, K_HOST * lax.axis_size("hst")),
        "hst",
        scatter_dimension=0,
        tiled=True,
    )
    squares = lax.psum(jnp.sum(shares * shares, axis=1), "chip")
    factor = lax.rsqrt(squares / feature_count + EPSILON)
    centroids = (shares * factor[:, None]).astype(jnp.bfloat16)
    own_block = lax.all_gather(centroids, "chip", axis=1, tiled=True)
    widened = points.astype(jnp.float32)
    unit_points = (
        widened * lax.rsqrt(jnp.mean(widened * widened, axis=1, keepdims=True) + EPSILON)
    ).astype(jnp.bfloat16)

    def nearest_in(candidates):
        scores = jnp.einsum(
            "pd,kd->pk", unit_points, candidates, preferred_element_type=jnp.float32
        )
        return jnp.min(2.0 - 2.0 * scores / feature_count, axis=1)

    nearest = nearest_in(own_block)
    moving = own_block
    for section_index in range(CYCLE - 1):
        moving = shifted(moving, "hst", 1)
        nearest = jnp.minimum(nearest, nearest_in(moving))
    return (centroids, nearest)


def solution(mesh):
    in_specs = (P(("hst", "chip"), None), P(("hst", "chip")))
    out_specs = (P("hst", "chip"), P(("hst", "chip")))
    return jax.shard_map(body, mesh=mesh, in_specs=in_specs, out_specs=out_specs, check_vma=False)
```

profile of v0, /device:TPU:0, one launch (start us, length us, event | category | flops | bytes accessed | tf_op | source)
XLA Modules:
  0.0 626.2 jit_solution(5738999434727934108)
XLA Ops:
  7.2 0.7 all-gather.3.cloned.1.call-update
  8.0 9.2 %all-gather = s32[4,1,512]{2,1,0:T(1,128)S(1)} all-gather(s32[1,1,512]{2,1,0:T(1,128)} %bitcast.25), channel_id=1, replica_groups=mesh['hst'=64,'chip'=4] {'chip'}, dimensions={0}, use_global_device_ids=true | all-gather | bytes 10240 | tf_op jit(solution)/shard_map/all_gather | solution.py:36
  17.2 60.4 %all-gather.3.cloned.1.call-done = bf16[2048,1024]{1,0:T(8,128)(2,1)} async-done(((bf16[512,1024]{1,0:T(8,128)(2,1)}), bf16[2048,1024]{1,0:T(8,128)(2,1)}) %all-gather.3.cloned.1.call-update) | async-done | bytes 4194320 | tf_op jit(solution)/shard_map/all_gather | solution.py:35
  77.6 1.3 constant_dynamic-slice_fusion
  78.9 28.5 %while.10 = (s32[]{:T(128)}, f32[8,1024,256]{2,1,0:T(8,128)}, s32[8]{0:T(128)S(1)}, s32[2048]{0:T(1024)S(1)}, bf16[2048,256]{1,0:T(8,128)(2,1)S(1)}, /*index=5*/s32[]{:T(128)}) while((s32[]{:T(128)}, f32[8,1024,256]{2,1,0:T(8,128)}, s32[8]{0:T(128)S(1)}, s32[2048]{0:T(1024)S(1)}, bf16[2048,256]{1,0:T(8,128)(2,1)S(1)}, ...), condition=%wide.region_1.2_spmd, body=%wide.region_0.1_spmd.sunk | while | flops 1075840000 | bytes 2114133 | solution.py:26
  79.5 0.6 iota_add_fusion.2
  80.1 2.3 fusion.50
  83.0 0.6 iota_add_fusion.2
  83.7 2.4 fusion.50
  86.6 0.6 iota_add_fusion.2
  87.3 2.3 fusion.50
  90.2 0.6 iota_add_fusion.2
  90.8 2.3 fusion.50
  93.7 0.6 iota_add_fusion.2
  94.4 2.3 fusion.50
  97.3 0.6 iota_add_fusion.2
  97.9 2.3 fusion.50
  101.5 2.3 fusion.50
  104.4 0.6 iota_add_fusion.2
  105.1 2.3 fusion.50
  107.4 398.8 %reduce-scatter.2.cloned.1.call-done = f32[128,256]{1,0:T(8,128)} async-done(((f32[8192,256]{1,0:T(8,128)}), f32[128,256]{1,0:T(8,128)}) %reduce-scatter.2.cloned.1.call-update) | async-done | bytes 131088 | tf_op jit(solution)/shard_map/reduce_scatter | solution.py:39
  506.2 1.0 multiply_reduce_fusion
  507.2 9.6 %psum.7 = f32[128]{0:T(128)S(1)} all-reduce(f32[128]{0:T(128)S(1)} %multiply_reduce_fusion), channel_id=1, replica_groups=mesh['hst'=64,'chip'=4] {'chip'}, use_global_device_ids=true, to_apply=%region_4.5 | all-reduce | flops 128 | bytes 1024 | tf_op jit(solution)/shard_map/psum | solution.py:45
  516.8 1.0 multiply_convert_fusion
  517.8 9.7 %all_gather.11 = bf16[128,1024]{1,0:T(8,128)(2,1)S(1)} all-gather(bf16[128,256]{1,0:T(8,128)(2,1)S(1)} %multiply_convert_fusion), channel_id=1, replica_groups=mesh['hst'=64,'chip'=4] {'chip'}, dimensions={1}, use_global_device_ids=true | all-gather | bytes 327680 | tf_op jit(solution)/shard_map/all_gather | solution.py:48
  527.5 14.6 %collective-permute-done = bf16[128,1024]{1,0:T(8,128)(2,1)S(1)} collective-permute-done((bf16[128,1024]{1,0:T(8,128)(2,1)S(1)}, bf16[128,1024]{1,0:T(8,128)(2,1)S(1)}, u32[]{:S(2)}, u32[]{:S(2)}) %collective-permute-start) | collective-permute-done | bytes 262176 | tf_op jit(solution)/shard_map/ppermute | solution.py:14
  542.0 13.7 %collective-permute-done.1 = bf16[128,1024]{1,0:T(8,128)(2,1)S(1)} collective-permute-done((bf16[128,1024]{1,0:T(8,128)(2,1)S(1)}, bf16[128,1024]{1,0:T(8,128)(2,1)S(1)}, u32[]{:S(2)}, u32[]{:S(2)}) %collective-permute-start.1) | collective-permute-done | bytes 262176 | tf_op jit(solution)/shard_map/ppermute | solution.py:14
  556.0 12.6 %collective-permute-done.2 = bf16[128,1024]{1,0:T(8,128)(2,1)S(1)} collective-permute-done((bf16[128,1024]{1,0:T(8,128)(2,1)S(1)}, bf16[128,1024]{1,0:T(8,128)(2,1)S(1)}, u32[]{:S(2)}, u32[]{:S(2)}) %collective-permute-start.2) | collective-permute-done | bytes 262176 | tf_op jit(solution)/shard_map/ppermute | solution.py:14
  569.2 11.8 %collective-permute-done.3 = bf16[128,1024]{1,0:T(8,128)(2,1)S(1)} collective-permute-done((bf16[128,1024]{1,0:T(8,128)(2,1)S(1)}, bf16[128,1024]{1,0:T(8,128)(2,1)S(1)}, u32[]{:S(2)}, u32[]{:S(2)}) %collective-permute-start.3) | collective-permute-done | bytes 262176 | tf_op jit(solution)/shard_map/ppermute | solution.py:14
  582.2 11.2 %collective-permute-done.4 = bf16[128,1024]{1,0:T(8,128)(2,1)S(1)} collective-permute-done((bf16[128,1024]{1,0:T(8,128)(2,1)S(1)}, bf16[128,1024]{1,0:T(8,128)(2,1)S(1)}, u32[]{:S(2)}, u32[]{:S(2)}) %collective-permute-start.4) | collective-permute-done | bytes 262176 | tf_op jit(solution)/shard_map/ppermute | solution.py:14
  594.5 11.2 %collective-permute-done.5 = bf16[128,1024]{1,0:T(8,128)(2,1)S(1)} collective-permute-done((bf16[128,1024]{1,0:T(8,128)(2,1)S(1)}, bf16[128,1024]{1,0:T(8,128)(2,1)S(1)}, u32[]{:S(2)}, u32[]{:S(2)}) %collective-permute-start.5) | collective-permute-done | bytes 262176 | tf_op jit(solution)/shard_map/ppermute | solution.py:14
  606.9 11.2 %collective-permute-done.6 = bf16[128,1024]{1,0:T(8,128)(2,1)S(1)} collective-permute-done((bf16[128,1024]{1,0:T(8,128)(2,1)S(1)}, bf16[128,1024]{1,0:T(8,128)(2,1)S(1)}, u32[]{:S(2)}, u32[]{:S(2)}) %collective-permute-start.6) | collective-permute-done | bytes 262176 | tf_op jit(solution)/shard_map/ppermute | solution.py:14
  (37 shorter events, 10.9 us)
Async XLA Ops:
  7.2 70.4 %all-gather.3.cloned.1.call-start = ((), (), s32[]{:S(2)}) async-start(), calls=%async_computation.1 | async-start | bytes 5242880 | tf_op jit(solution)/shard_map/all_gather | solution.py:35
  7.9 498.3 %reduce-scatter.2.cloned.1.call-start = ((), (), s32[]{:S(2)}) async-start(), calls=%async_computation.2 | async-start | bytes 8519680 | tf_op jit(solution)/shard_map/reduce_scatter | solution.py:39
  107.4 448.4 %copy-start = (bf16[512,1024]{1,0:T(8,128)(2,1)S(1)}, bf16[512,1024]{1,0:T(8,128)(2,1)}, u32[]{:S(2)}) copy-start(bf16[512,1024]{1,0:T(8,128)(2,1)} %param.4) | copy-start | bytes 3145732
  517.8 63.8 %copy-start.1 = (bf16[128,256]{1,0:T(8,128)(2,1)}, bf16[128,256]{1,0:T(8,128)(2,1)S(1)}, u32[]{:S(2)}) copy-start(bf16[128,256]{1,0:T(8,128)(2,1)S(1)} %multiply_convert_fusion) | copy-start | bytes 196612
  527.5 14.6 %collective-permute-start = (bf16[128,1024]{1,0:T(8,128)(2,1)S(1)}, bf16[128,1024]{1,0:T(8,128)(2,1)S(1)}, u32[]{:S(2)}, u32[]{:S(2)}) collective-permute-start(bf16[128,1024]{1,0:T(8,128)(2,1)S(1)} %all_gather.11), channel_id=1, source_target_pairs={{252,0},{0,4},{4,8},{8,12},{12,16},{16,20},{20,24},{24,28},{28,32}... | collective-permute-start | bytes 786440 | tf_op jit(solution)/shard_map/ppermute | solution.py:14
  542.0 13.7 %collective-permute-start.1 = (bf16[128,1024]{1,0:T(8,128)(2,1)S(1)}, bf16[128,1024]{1,0:T(8,128)(2,1)S(1)}, u32[]{:S(2)}, u32[]{:S(2)}) collective-permute-start(bf16[128,1024]{1,0:T(8,128)(2,1)S(1)} %collective-permute-done), channel_id=1, source_target_pairs={{252,0},{0,4},{4,8},{8,12},{12,16},{16,20},{20,24},{24,28},{28,32}... | collective-permute-start | bytes 786440 | tf_op jit(solution)/shard_map/ppermute | solution.py:14
  555.7 12.9 %collective-permute-start.2 = (bf16[128,1024]{1,0:T(8,128)(2,1)S(1)}, bf16[128,1024]{1,0:T(8,128)(2,1)S(1)}, u32[]{:S(2)}, u32[]{:S(2)}) collective-permute-start(bf16[128,1024]{1,0:T(8,128)(2,1)S(1)} %collective-permute-done.1), channel_id=1, source_target_pairs={{252,0},{0,4},{4,8},{8,12},{12,16},{16,20},{20,24},{24,28},{28,32}... | collective-permute-start | bytes 786440 | tf_op jit(solution)/shard_map/ppermute | solution.py:14
  568.6 12.4 %collective-permute-start.3 = (bf16[128,1024]{1,0:T(8,128)(2,1)S(1)}, bf16[128,1024]{1,0:T(8,128)(2,1)S(1)}, u32[]{:S(2)}, u32[]{:S(2)}) collective-permute-start(bf16[128,1024]{1,0:T(8,128)(2,1)S(1)} %collective-permute-done.2), channel_id=1, source_target_pairs={{252,0},{0,4},{4,8},{8,12},{12,16},{16,20},{20,24},{24,28},{28,32}... | collective-permute-start | bytes 786440 | tf_op jit(solution)/shard_map/ppermute | solution.py:14
  581.0 12.4 %collective-permute-start.4 = (bf16[128,1024]{1,0:T(8,128)(2,1)S(1)}, bf16[128,1024]{1,0:T(8,128)(2,1)S(1)}, u32[]{:S(2)}, u32[]{:S(2)}) collective-permute-start(bf16[128,1024]{1,0:T(8,128)(2,1)S(1)} %collective-permute-done.3), channel_id=1, source_target_pairs={{252,0},{0,4},{4,8},{8,12},{12,16},{16,20},{20,24},{24,28},{28,32}... | collective-permute-start | bytes 786440 | tf_op jit(solution)/shard_map/ppermute | solution.py:14
  593.4 12.4 %collective-permute-start.5 = (bf16[128,1024]{1,0:T(8,128)(2,1)S(1)}, bf16[128,1024]{1,0:T(8,128)(2,1)S(1)}, u32[]{:S(2)}, u32[]{:S(2)}) collective-permute-start(bf16[128,1024]{1,0:T(8,128)(2,1)S(1)} %collective-permute-done.4), channel_id=1, source_target_pairs={{252,0},{0,4},{4,8},{8,12},{12,16},{16,20},{20,24},{24,28},{28,32}... | collective-permute-start | bytes 786440 | tf_op jit(solution)/shard_map/ppermute | solution.py:14
  605.8 12.4 %collective-permute-start.6 = (bf16[128,1024]{1,0:T(8,128)(2,1)S(1)}, bf16[128,1024]{1,0:T(8,128)(2,1)S(1)}, u32[]{:S(2)}, u32[]{:S(2)}) collective-permute-start(bf16[128,1024]{1,0:T(8,128)(2,1)S(1)} %collective-permute-done.5), channel_id=1, source_target_pairs={{252,0},{0,4},{4,8},{8,12},{12,16},{16,20},{20,24},{24,28},{28,32}... | collective-permute-start | bytes 786440 | tf_op jit(solution)/shard_map/ppermute | solution.py:14
Sparse Core Ops, SparseCore 0:
  9.8 67.7 all-gather.2
  107.5 398.6 reduce-scatter.1
where the time goes:
time: 626 us
  waiting for transfers between devices  546 us (87%)
  blocking collectives  28.5 us (5%)
  matrix products  23.1 us (4%)
  between operations  14.1 us (2%)
  other arithmetic  8.06 us (1%)
    reduce_scatter x1, waiting for transfers between devices, body(): lax.psum_scatter(cluster_sums(columns, host_labels, K_HOST * lax.axis_siz...  399 us
    ppermute x7, waiting for transfers between devices, shifted(): return lax.ppermute(block, axis, route)  86.4 us
    all_gather x1, waiting for transfers between devices, body(): lax.all_gather(points, 'chip', axis=0, tiled=True)  60.4 us
    dot_general x8, matrix products, one_block(): return jnp.dot(member, values, preferred_element_type=jnp.float32)  18.6 us
  transfers between devices with their start and end apart: 9, of which 9 were waited for; matrix products, arithmetic and copies ran while one was open for 1% of the time, Pallas kernels for 0%

commit v1 on v0

--- a/solution.py
+++ b/solution.py
@@ -32,7 +32,9 @@
     chip_index = lax.axis_index("chip")
     quarter = feature_count // chip_count
     host_points, host_labels = (
-        lax.all_gather(points, "chip", axis=0, tiled=True),
+        jnp.concatenate(
+            lax.all_to_all(jnp.stack([points] * lax.axis_size("chip")), "chip", 0, 0), axis=0
+        ),
         lax.all_gather(assign, "chip", axis=0, tiled=True),
     )
     columns = lax.dynamic_slice_in_dim(host_points, chip_index * quarter, quarter, 1)

time: 626 us -> 668 us (1.067)
  blocking collectives: 28.5 us -> 117 us
  waiting for transfers between devices: 546 us -> 489 us
  starting transfers between devices: 0.09 us -> 6.9 us
    all_gather x1, blocking collectives: 9.23 us -> 97.6 us  [body(): lax.all_gather(assign, 'chip', axis=0, tiled=True)]
    all_gather x1 -> x0, waiting for transfers between devices: 60.4 us -> none  [body(): lax.all_gather(points, 'chip', axis=0, tiled=True)]
    all_to_all x0 -> x1, starting transfers between devices: none -> 6.88 us  [body(): lax.all_to_all(jnp.stack([points] * lax.axis_size('chip')), 'chip', 0, 0)]
  transfers between devices with their start and end apart: 9 -> 9, of which waited for: 9 -> 8; matrix products, arithmetic and copies ran while one was open for 1% -> 1% of each run, Pallas kernels for 0% -> 0%
where the time goes in v1:
time: 668 us
  waiting for transfers between devices  489 us (73%)
  blocking collectives  117 us (18%)
  matrix products  23.2 us (3%)
  between operations  14.1 us (2%)
  local copies, waits for them, and re-layouts  9.7 us (1%)
  other arithmetic  8.06 us (1%)
  starting transfers between devices  6.9 us (1%)
    reduce_scatter x1, waiting for transfers between devices, body(): lax.psum_scatter(cluster_sums(columns, host_labels, K_HOST * lax.axis_siz...  403 us
    all_gather x1, blocking collectives, body(): lax.all_gather(assign, 'chip', axis=0, tiled=True)  97.6 us
    ppermute x7, waiting for transfers between devices, shifted(): return lax.ppermute(block, axis, route)  86.3 us
    dot_general x8, matrix products, one_block(): return jnp.dot(member, values, preferred_element_type=jnp.float32)  18.6 us
  transfers between devices with their start and end apart: 9, of which 8 were waited for; matrix products, arithmetic and copies ran while one was open for 1% of the time, Pallas kernels for 0%

profile of v1, /device:TPU:0, one launch (start us, length us, event | category | flops | bytes accessed | tf_op | source)
XLA Modules:
  0.0 668.0 jit_solution(3677720346168061699)
XLA Ops:
  7.2 3.7 stack.2
  10.9 6.9 %all-to-all-start = ((bf16[4,512,1024]{2,1,0:T(8,128)(2,1)}), bf16[4,512,1024]{2,1,0:T(8,128)(2,1)}, u32[]{:S(2)}, u32[]{:S(2)}) async-start(bf16[4,512,1024]{2,1,0:T(8,128)(2,1)} %stack.2), calls=%async_computation | async-start | bytes 8388608 | tf_op jit(solution)/shard_map/all_to_all | solution.py:36
  17.8 97.6 %all-gather = s32[4,1,512]{2,1,0:T(1,128)S(1)} all-gather(s32[1,1,512]{2,1,0:T(1,128)S(1)} %bitcast.26), channel_id=1, replica_groups=mesh['hst'=64,'chip'=4] {'chip'}, dimensions={0}, use_global_device_ids=true | all-gather | bytes 10240 | tf_op jit(solution)/shard_map/all_gather | solution.py:38
  115.3 1.3 constant_dynamic-slice_fusion
  116.6 28.5 %while.10 = (s32[]{:T(128)}, f32[8,1024,256]{2,1,0:T(8,128)}, s32[8]{0:T(128)S(1)}, s32[2048]{0:T(1024)S(1)}, bf16[2048,256]{1,0:T(8,128)(2,1)S(1)}, /*index=5*/s32[]{:T(128)}) while((s32[]{:T(128)}, f32[8,1024,256]{2,1,0:T(8,128)}, s32[8]{0:T(128)S(1)}, s32[2048]{0:T(1024)S(1)}, bf16[2048,256]{1,0:T(8,128)(2,1)S(1)}, ...), condition=%wide.region_1.2_spmd, body=%wide.region_0.1_spmd.sunk | while | flops 1075840000 | bytes 2114133 | solution.py:26
  117.2 0.6 iota_add_fusion.2
  117.9 2.3 fusion.50
  120.8 0.6 iota_add_fusion.2
  121.4 2.4 fusion.50
  124.4 0.6 iota_add_fusion.2
  125.0 2.3 fusion.50
  127.9 0.6 iota_add_fusion.2
  128.6 2.3 fusion.50
  131.5 0.6 iota_add_fusion.2
  132.1 2.3 fusion.50
  135.0 0.6 iota_add_fusion.2
  135.7 2.3 fusion.50
  139.3 2.3 fusion.50
  142.2 0.6 iota_add_fusion.2
  142.8 2.3 fusion.50
  145.1 402.8 %reduce-scatter.2.cloned.1.call-done = f32[128,256]{1,0:T(8,128)} async-done(((f32[8192,256]{1,0:T(8,128)}), f32[128,256]{1,0:T(8,128)}) %reduce-scatter.2.cloned.1.call-update) | async-done | bytes 131088 | tf_op jit(solution)/shard_map/reduce_scatter | solution.py:41
  548.0 1.0 multiply_reduce_fusion
  549.0 9.6 %psum.7 = f32[128]{0:T(128)S(1)} all-reduce(f32[128]{0:T(128)S(1)} %multiply_reduce_fusion), channel_id=1, replica_groups=mesh['hst'=64,'chip'=4] {'chip'}, use_global_device_ids=true, to_apply=%region_4.5 | all-reduce | flops 128 | bytes 1024 | tf_op jit(solution)/shard_map/psum | solution.py:47
  558.6 1.0 multiply_convert_fusion
  559.6 9.7 %all_gather.7 = bf16[128,1024]{1,0:T(8,128)(2,1)S(1)} all-gather(bf16[128,256]{1,0:T(8,128)(2,1)S(1)} %multiply_convert_fusion), channel_id=1, replica_groups=mesh['hst'=64,'chip'=4] {'chip'}, dimensions={1}, use_global_device_ids=true | all-gather | bytes 327680 | tf_op jit(solution)/shard_map/all_gather | solution.py:50
  569.3 14.6 %collective-permute-done = bf16[128,1024]{1,0:T(8,128)(2,1)S(1)} collective-permute-done((bf16[128,1024]{1,0:T(8,128)(2,1)S(1)}, bf16[128,1024]{1,0:T(8,128)(2,1)S(1)}, u32[]{:S(2)}, u32[]{:S(2)}) %collective-permute-start) | collective-permute-done | bytes 262176 | tf_op jit(solution)/shard_map/ppermute | solution.py:14
  583.8 13.7 %collective-permute-done.1 = bf16[128,1024]{1,0:T(8,128)(2,1)S(1)} collective-permute-done((bf16[128,1024]{1,0:T(8,128)(2,1)S(1)}, bf16[128,1024]{1,0:T(8,128)(2,1)S(1)}, u32[]{:S(2)}, u32[]{:S(2)}) %collective-permute-start.1) | collective-permute-done | bytes 262176 | tf_op jit(solution)/shard_map/ppermute | solution.py:14
  597.8 12.6 %collective-permute-done.2 = bf16[128,1024]{1,0:T(8,128)(2,1)S(1)} collective-permute-done((bf16[128,1024]{1,0:T(8,128)(2,1)S(1)}, bf16[128,1024]{1,0:T(8,128)(2,1)S(1)}, u32[]{:S(2)}, u32[]{:S(2)}) %collective-permute-start.2) | collective-permute-done | bytes 262176 | tf_op jit(solution)/shard_map/ppermute | solution.py:14
  611.0 11.8 %collective-permute-done.3 = bf16[128,1024]{1,0:T(8,128)(2,1)S(1)} collective-permute-done((bf16[128,1024]{1,0:T(8,128)(2,1)S(1)}, bf16[128,1024]{1,0:T(8,128)(2,1)S(1)}, u32[]{:S(2)}, u32[]{:S(2)}) %collective-permute-start.3) | collective-permute-done | bytes 262176 | tf_op jit(solution)/shard_map/ppermute | solution.py:14
  624.0 11.2 %collective-permute-done.4 = bf16[128,1024]{1,0:T(8,128)(2,1)S(1)} collective-permute-done((bf16[128,1024]{1,0:T(8,128)(2,1)S(1)}, bf16[128,1024]{1,0:T(8,128)(2,1)S(1)}, u32[]{:S(2)}, u32[]{:S(2)}) %collective-permute-start.4) | collective-permute-done | bytes 262176 | tf_op jit(solution)/shard_map/ppermute | solution.py:14
  636.4 11.2 %collective-permute-done.5 = bf16[128,1024]{1,0:T(8,128)(2,1)S(1)} collective-permute-done((bf16[128,1024]{1,0:T(8,128)(2,1)S(1)}, bf16[128,1024]{1,0:T(8,128)(2,1)S(1)}, u32[]{:S(2)}, u32[]{:S(2)}) %collective-permute-start.5) | collective-permute-done | bytes 262176 | tf_op jit(solution)/shard_map/ppermute | solution.py:14
  648.7 11.2 %collective-permute-done.6 = bf16[128,1024]{1,0:T(8,128)(2,1)S(1)} collective-permute-done((bf16[128,1024]{1,0:T(8,128)(2,1)S(1)}, bf16[128,1024]{1,0:T(8,128)(2,1)S(1)}, u32[]{:S(2)}, u32[]{:S(2)}) %collective-permute-start.6) | collective-permute-done | bytes 262176 | tf_op jit(solution)/shard_map/ppermute | solution.py:14
  (39 shorter events, 10.8 us)
Async XLA Ops:
  10.9 6.9 %copy-start.2 = (s32[512]{0:T(512)S(1)}, s32[512]{0:T(512)}, u32[]{:S(2)}) copy-start(s32[512]{0:T(512)} %param.5) | copy-start | bytes 6148
  10.9 104.5 %all-to-all-start = ((bf16[4,512,1024]{2,1,0:T(8,128)(2,1)}), bf16[4,512,1024]{2,1,0:T(8,128)(2,1)}, u32[]{:S(2)}, u32[]{:S(2)}) async-start(bf16[4,512,1024]{2,1,0:T(8,128)(2,1)} %stack.2), calls=%async_computation | async-start | bytes 8388608 | tf_op jit(solution)/shard_map/all_to_all | solution.py:36
  17.8 530.2 %reduce-scatter.2.cloned.1.call-start = ((), (), s32[]{:S(2)}) async-start(), calls=%async_computation.2 | async-start | bytes 8519680 | tf_op jit(solution)/shard_map/reduce_scatter | solution.py:41
  145.1 452.4 %copy-start = (bf16[512,1024]{1,0:T(8,128)(2,1)S(1)}, bf16[512,1024]{1,0:T(8,128)(2,1)}, u32[]{:S(2)}) copy-start(bf16[512,1024]{1,0:T(8,128)(2,1)} %param.4) | copy-start | bytes 3145732
  559.6 63.8 %copy-start.1 = (bf16[128,256]{1,0:T(8,128)(2,1)}, bf16[128,256]{1,0:T(8,128)(2,1)S(1)}, u32[]{:S(2)}) copy-start(bf16[128,256]{1,0:T(8,128)(2,1)S(1)} %multiply_convert_fusion) | copy-start | bytes 196612
  569.3 14.6 %collective-permute-start = (bf16[128,1024]{1,0:T(8,128)(2,1)S(1)}, bf16[128,1024]{1,0:T(8,128)(2,1)S(1)}, u32[]{:S(2)}, u32[]{:S(2)}) collective-permute-start(bf16[128,1024]{1,0:T(8,128)(2,1)S(1)} %all_gather.7), channel_id=1, source_target_pairs={{252,0},{0,4},{4,8},{8,12},{12,16},{16,20},{20,24},{24,28},{28,32}... | collective-permute-start | bytes 786440 | tf_op jit(solution)/shard_map/ppermute | solution.py:14
  583.8 13.7 %collective-permute-start.1 = (bf16[128,1024]{1,0:T(8,128)(2,1)S(1)}, bf16[128,1024]{1,0:T(8,128)(2,1)S(1)}, u32[]{:S(2)}, u32[]{:S(2)}) collective-permute-start(bf16[128,1024]{1,0:T(8,128)(2,1)S(1)} %collective-permute-done), channel_id=1, source_target_pairs={{252,0},{0,4},{4,8},{8,12},{12,16},{16,20},{20,24},{24,28},{28,32}... | collective-permute-start | bytes 786440 | tf_op jit(solution)/shard_map/ppermute | solution.py:14
  597.6 12.9 %collective-permute-start.2 = (bf16[128,1024]{1,0:T(8,128)(2,1)S(1)}, bf16[128,1024]{1,0:T(8,128)(2,1)S(1)}, u32[]{:S(2)}, u32[]{:S(2)}) collective-permute-start(bf16[128,1024]{1,0:T(8,128)(2,1)S(1)} %collective-permute-done.1), channel_id=1, source_target_pairs={{252,0},{0,4},{4,8},{8,12},{12,16},{16,20},{20,24},{24,28},{28,32}... | collective-permute-start | bytes 786440 | tf_op jit(solution)/shard_map/ppermute | solution.py:14
  610.4 12.4 %collective-permute-start.3 = (bf16[128,1024]{1,0:T(8,128)(2,1)S(1)}, bf16[128,1024]{1,0:T(8,128)(2,1)S(1)}, u32[]{:S(2)}, u32[]{:S(2)}) collective-permute-start(bf16[128,1024]{1,0:T(8,128)(2,1)S(1)} %collective-permute-done.2), channel_id=1, source_target_pairs={{252,0},{0,4},{4,8},{8,12},{12,16},{16,20},{20,24},{24,28},{28,32}... | collective-permute-start | bytes 786440 | tf_op jit(solution)/shard_map/ppermute | solution.py:14
  622.8 12.4 %collective-permute-start.4 = (bf16[128,1024]{1,0:T(8,128)(2,1)S(1)}, bf16[128,1024]{1,0:T(8,128)(2,1)S(1)}, u32[]{:S(2)}, u32[]{:S(2)}) collective-permute-start(bf16[128,1024]{1,0:T(8,128)(2,1)S(1)} %collective-permute-done.3), channel_id=1, source_target_pairs={{252,0},{0,4},{4,8},{8,12},{12,16},{16,20},{20,24},{24,28},{28,32}... | collective-permute-start | bytes 786440 | tf_op jit(solution)/shard_map/ppermute | solution.py:14
  635.2 12.4 %collective-permute-start.5 = (bf16[128,1024]{1,0:T(8,128)(2,1)S(1)}, bf16[128,1024]{1,0:T(8,128)(2,1)S(1)}, u32[]{:S(2)}, u32[]{:S(2)}) collective-permute-start(bf16[128,1024]{1,0:T(8,128)(2,1)S(1)} %collective-permute-done.4), channel_id=1, source_target_pairs={{252,0},{0,4},{4,8},{8,12},{12,16},{16,20},{20,24},{24,28},{28,32}... | collective-permute-start | bytes 786440 | tf_op jit(solution)/shard_map/ppermute | solution.py:14
  647.6 12.4 %collective-permute-start.6 = (bf16[128,1024]{1,0:T(8,128)(2,1)S(1)}, bf16[128,1024]{1,0:T(8,128)(2,1)S(1)}, u32[]{:S(2)}, u32[]{:S(2)}) collective-permute-start(bf16[128,1024]{1,0:T(8,128)(2,1)S(1)} %collective-permute-done.5), channel_id=1, source_target_pairs={{252,0},{0,4},{4,8},{8,12},{12,16},{16,20},{20,24},{24,28},{28,32}... | collective-permute-start | bytes 786440 | tf_op jit(solution)/shard_map/ppermute | solution.py:14
Sparse Core Ops, SparseCore 0:
  145.3 402.6 reduce-scatter.1
